TPU v7x, 32 devices: a whole 2x2x4 slice. The times are simulated.
32 devices in a mesh: seq: 8 (over z, x), head: 4 (over y, core).
Axes of the slice: x: 2, y: 2, z: 4, core: 2. Of those that a mesh axis runs over, the one named last changes fastest.
Arguments:
- queries: float32 [8192, 2048], P('seq', 'head')
- keys: float32 [8192, 2048], P('seq', 'head')
- values: float32 [8192, 2048], P('seq', 'head'), may hold values from -6 to 6
- positions: int32 [8192], P('seq'), may hold values from 0 to 8191, as said below
- cluster: int32 [8192], P('seq'), may hold values from 0 to 7, as said below
- slot: int32 [8192], P('seq'), may hold values from 0 to 1023, as said below
- out_weight: float32 [2048, 4096], P('head'), may hold values from -0.5 to 0.5
Outputs:
- projected: float32 [8192, 4096], P('seq', 'head')
Inputs may be any that keep to these rules, and one draw needn't show every extreme that they name: Every cluster holds exactly 1024 tokens. Of the tokens of one index of seq, at most 192 have cluster ids in one range k * 1 to (k + 1) - 1. Within each cluster every slot is taken once, in increasing order of position. `positions`: each position is taken by exactly one token.
All inputs are finite; a program needn't handle non-finite values.
Results may differ from a plain program's by a relative error of at most 0.0003.
Values sent between devices are 32-bit elements; how exact they have to be, the bound alone decides.
No kernel may reach another device: no remote copies, remote signals or barrier semaphores. Data moves between devices by JAX's collectives and lax.ppermute only.
A program may use at most 128 MiB of HBM per device.

v0:
```python
import math
import jax
import jax.numpy as jnp
from jax import lax
from jax.sharding import PartitionSpec as P

DH = 128
CS = 1024
CL_DEV = 1
ROPE_BASE = 500000.0
ORIG_CONTEXT = 8192.0
STRETCH = 4.0
BETA_FAST = 32.0
BETA_SLOW = 1.0


def yarn_tables(token_pos, width):
    half_width = width // 2
    expo = jnp.arange(half_width, dtype=jnp.float32) * 2.0 / width
    theta = jnp.exp(-expo * math.log(ROPE_BASE))
    ratio = ORIG_CONTEXT * theta / (2.0 * math.pi)
    ramp = jnp.clip((ratio - BETA_SLOW) / (BETA_FAST - BETA_SLOW), 0.0, 1.0)
    freq = theta * (ramp + (1.0 - ramp) / STRETCH)
    angle = token_pos.astype(jnp.float32)[:, None] * freq[None, :]
    mscale = 0.1 * math.log(STRETCH) + 1.0
    cos_table = jnp.concatenate([jnp.cos(angle), jnp.cos(angle)], -1) * mscale
    sin_table = jnp.concatenate([jnp.sin(angle), jnp.sin(angle)], -1) * mscale
    return (cos_table[:, None, :], sin_table[:, None, :])


def rotate(field, cos_table, sin_table):
    half_width = field.shape[-1] // 2
    turned = jnp.concatenate([-field[..., half_width:], field[..., :half_width]], -1)
    return field * cos_table + turned * sin_table


def cluster_attention(triple):
    query_c, key_c, value_c = triple
    length = query_c.shape[0]
    scores = jnp.einsum(
        "qhd,khd->hqk", query_c, key_c, precision=lax.Precision.HIGHEST
    ) / math.sqrt(query_c.shape[-1])
    causal = jnp.arange(length)[:, None] >= jnp.arange(length)[None, :]
    scores = jnp.where(causal[None], scores, -jnp.inf)
    peak = jnp.max(scores, -1, keepdims=True)
    weights = jnp.exp(scores - peak)
    total = jnp.sum(weights, -1, keepdims=True)
    summed = jnp.einsum("hqk,khd->qhd", weights, value_c, precision=lax.Precision.HIGHEST)
    return summed / jnp.transpose(total, (1, 0, 2))


def attend_local(query_all, key_all, value_all):
    row_count, head_count, width = query_all.shape
    grouped = (
        query_all.reshape(row_count // CS, CS, head_count, width),
        key_all.reshape(row_count // CS, CS, head_count, width),
        value_all.reshape(row_count // CS, CS, head_count, width),
    )
    return lax.map(cluster_attention, grouped).reshape(row_count, head_count, width)


def per_device(queries, keys, values, positions, cluster, slot, out_weight):
    seq_count = lax.axis_size("seq")
    head_count = lax.axis_size("head")
    head_index = lax.axis_index("head")
    col_width = out_weight.shape[1] // head_count
    weight_blocks = out_weight.reshape(out_weight.shape[0], head_count, col_width)
    weight_parts = [None] * head_count
    for shift in range(head_count):
        if shift == 0:
            piece = weight_blocks[:, head_index]
        else:
            dest = (head_index + shift) % head_count
            piece = lax.ppermute(
                jnp.take(weight_blocks, dest, axis=1),
                "head",
                [(src, (src + shift) % head_count) for src in range(head_count)],
            )
        weight_parts[shift] = piece
    stacked_w = jnp.stack(weight_parts, 0)
    order = (head_index - jnp.arange(head_count)) % head_count
    weight_cols = stacked_w[order].reshape(head_count * out_weight.shape[0], col_width)
    row_count = queries.shape[0]
    capacity = 3 * row_count // (2 * seq_count)
    buffer_rows = seq_count * capacity
    heads_here = queries.shape[1] // DH
    owner_ids = cluster // CL_DEV
    target_row = cluster % CL_DEV * CS + slot
    one_hot = (owner_ids[:, None] == jnp.arange(seq_count)[None, :]).astype(jnp.int32)
    token_rank = jnp.sum(jnp.cumsum(one_hot, 0) * one_hot, 1) - 1
    send_row = owner_ids * capacity + token_rank
    source_token = (
        jnp.full((buffer_rows,), row_count, jnp.int32)
        .at[send_row]
        .set(jnp.arange(row_count, dtype=jnp.int32))
    )
    cos_table, sin_table = yarn_tables(positions, DH)
    shaped = (row_count, heads_here, DH)
    rot_q = rotate(queries.reshape(shaped), cos_table, sin_table)
    rot_k = rotate(keys.reshape(shaped), cos_table, sin_table)
    stacked = jnp.concatenate([rot_q, rot_k, values.reshape(shaped)], 1)
    stacked = jnp.concatenate([stacked, jnp.zeros((1, 3 * heads_here, DH), jnp.float32)], 0)
    send_all = stacked[source_token]
    send_q = send_all[:, :heads_here]
    send_k = send_all[:, heads_here : 2 * heads_here]
    send_v = send_all[:, 2 * heads_here :]
    slot_rows = jnp.full((buffer_rows,), row_count, jnp.int32).at[send_row].set(target_row)
    arrived = lax.all_to_all(slot_rows, "seq", split_axis=0, concat_axis=0, tiled=True)
    picked = jnp.minimum(arrived, row_count - 1)
    where_from = (
        jnp.zeros((row_count,), jnp.int32)
        .at[arrived]
        .set(jnp.arange(buffer_rows, dtype=jnp.int32), mode="drop")
    )

    def place(pieces):
        return pieces[where_from]

    received = (
        lax.all_to_all(send_q, "seq", split_axis=0, concat_axis=0, tiled=True),
        lax.all_to_all(send_k, "seq", split_axis=0, concat_axis=0, tiled=True),
        lax.all_to_all(send_v, "seq", split_axis=0, concat_axis=0, tiled=True),
    )
    result = attend_local(place(received[0]), place(received[1]), place(received[2]))
    result, weight_cols = lax.optimization_barrier((result, weight_cols))
    returned = lax.all_to_all(result[picked], "seq", split_axis=0, concat_axis=0, tiled=True)
    mixed = returned[send_row].reshape(row_count, heads_here * DH)
    gathered = lax.all_gather(mixed, "head", axis=1, tiled=True)
    projected = jnp.dot(
        gathered, weight_cols, precision=lax.Precision.HIGHEST, preferred_element_type=jnp.float32
    )
    return projected


def solution(mesh):
    in_specs = (
        P("seq", "head"),
        P("seq", "head"),
        P("seq", "head"),
        P("seq"),
        P("seq"),
        P("seq"),
        P("head", None),
    )
    out_specs = P("seq", "head")
    return jax.shard_map(
        per_device, mesh=mesh, in_specs=in_specs, out_specs=out_specs, check_vma=False
    )
```

profile of v0, /device:TPU:0, one launch (start us, length us, event | category | flops | bytes accessed | tf_op | source)
XLA Modules:
  0.0 617.9 jit_solution(9982841143723869538)
XLA Ops:
  6.5 0.7 fusion.19
  7.2 2.3 reduce-window.6
  9.5 0.3 slice_reduce_fusion
  9.8 0.2 reduce-window.9
  9.9 0.1 add_bitcast_fusion
  10.0 0.7 fusion.18
  10.7 0.7 broadcast_clamp_fusion
  11.4 4.5 scatter_custom_fusion.1
  15.9 0.7 all_to_all.27
  16.6 7.3 %all-to-all-start.1 = ((s32[8,192,1]{1,2,0:T(1,128)}), s32[8,192,1]{1,2,0:T(1,128)S(1)}, u32[]{:S(2)}, u32[]{:S(2)}) async-start(s32[8,192,1]{1,2,0:T(1,128)} %all_to_all.27), calls=%async_computation.1 | async-start | bytes 16384 | tf_op jit(solution)/shard_map/all_to_all | solution.py:108
  23.8 2.9 reshape.229
  26.7 1.9 reshape.228
  28.7 0.0 copy-start.5
  28.7 3.0 reshape.227
  31.6 0.0 copy-done.5
  31.6 4.8 scatter_custom_fusion
  36.5 4.6 slice_negate_fusion
  41.2 1.9 multiply_cosine_fusion
  43.1 0.3 maximum_multiply_fusion.2
  43.4 0.0 copy-start.3
  43.4 3.0 fusion.7
  46.5 5.3 select_maximum_fusion
  51.8 12.0 %gather_fusion = f32[1536,12,128]{2,1,0:T(8,128)} fusion(f32[1025,12,128]{2,1,0:T(8,128)} %select_maximum_fusion, s32[2048]{0:T(1024)S(1)} %pad_clamp_fusion.1), kind=kCustom, calls=%fused_computation | custom fusion | bytes 18880512 | tf_op jit(solution)/shard_map/gather | solution.py:103
  63.8 10.0 %fusion.33 = (f32[1536,4,128]{2,1,0:T(4,128)}, f32[1536,4,128]{2,1,0:T(4,128)}, f32[1536,4,128]{2,1,0:T(4,128)S(1)}) fusion(f32[1536,12,128]{2,1,0:T(8,128)} %gather_fusion), kind=kLoop, calls=%fused_computation.85 | loop fusion | bytes 18874368 | tf_op jit(solution)/shard_map/slice | solution.py:106
  73.8 0.0 all-to-all-done.1
  73.8 76.2 %all_to_all.33 = f32[1536,4,128]{2,1,0:T(4,128)} all-to-all(f32[1536,4,128]{2,1,0:T(4,128)S(1)} %get-tuple-element.42), channel_id=1, replica_groups=mesh['seq'=8,'head'=4] {'seq'}, dimensions={0} | all-to-all | bytes 6291456 | tf_op jit(solution)/shard_map/all_to_all | solution.py:121
  149.9 3.8 all-to-all-start.2
  153.8 10.8 %reshape.231 = f32[512,4,1024]{2,1,0:T(4,128)} reshape(f32[512,4096]{1,0:T(8,128)} %param.15) | data formatting | bytes 16777216 | tf_op jit(solution)/shard_map/reshape | solution.py:67
  164.6 59.2 %all-to-all-done.2 = f32[1536,4,128]{2,1,0:T(4,128)S(1)} async-done(((f32[1536,4,128]{2,1,0:T(4,128)}), f32[1536,4,128]{2,1,0:T(4,128)S(1)}, u32[]{:S(2)}, u32[]{:S(2)}) %all-to-all-start.2) | async-done | bytes 3145760 | tf_op jit(solution)/shard_map/all_to_all | solution.py:120
  223.8 1.7 copy-done.2
  225.5 4.5 all-to-all-start
  230.0 0.0 all-gather.2.cloned.1.call-start
  230.1 20.0 %constant_dynamic-slice_fusion.2 = (f32[512,1,1024]{2,1,0:T(1,128)}, f32[512,1,1024]{2,1,0:T(1,128)S(1)}, f32[512,1,1024]{2,1,0:T(1,128)S(1)}, f32[512,1,1024]{2,1,0:T(1,128)}) fusion(f32[512,4,1024]{2,1,0:T(4,128)} %reshape.231, s32[]{:T(128)S(6)} %select_n.98, s32[]{:T(128)S(6)} %select_n.115, s32[]{:T(128)S(6)} %select_n.119, pred[]{:T(512)S(6)} %and.53, ...), kind=kLoop, calls=%fused_computation.79 | loop fusion | flops 524288 | bytes 16777232 | tf_op jit(solution)/shard_map/dynamic_slice | solution.py:71
  250.1 1.8 copy.56
  251.9 0.0 collective-permute-start.2
  251.9 3.5 fusion.9
  255.4 1.5 collective-permute-start.1
  256.9 1.8 fusion.10
  258.7 0.2 collective-permute-start
  258.9 0.5 copy.57
  259.4 0.3 iota_compare_fusion.1
  259.8 0.1 all_to_all.23
  259.9 6.2 scatter_custom_fusion.2
  266.1 27.5 %collective-permute-done.2 = f32[512,1024]{1,0:T(8,128)} collective-permute-done((f32[512,1024]{1,0:T(8,128)}, f32[512,1024]{1,0:T(8,128)}, u32[]{:S(2)}, u32[]{:S(2)}) %collective-permute-start.2) | collective-permute-done | bytes 2097184 | tf_op jit(solution)/shard_map/ppermute | solution.py:74
  293.6 47.9 %collective-permute-done.1 = f32[512,1024]{1,0:T(8,128)} collective-permute-done((f32[512,1024]{1,0:T(8,128)}, f32[512,1024]{1,0:T(8,128)}, u32[]{:S(2)}, u32[]{:S(2)}) %collective-permute-start.1) | collective-permute-done | bytes 2097184 | tf_op jit(solution)/shard_map/ppermute | solution.py:74
  341.5 3.6 collective-permute-done
  345.1 5.8 pad_maximum_fusion
  350.9 7.7 %gather_fusion.4 = f32[4,512,1024]{2,1,0:T(8,128)} fusion(f32[4,512,1024]{2,1,0:T(8,128)} %pad_maximum_fusion, s32[1024]{0:T(1024)S(1)} %pad_clamp_fusion.2), kind=kCustom, calls=%fused_computation.4 | custom fusion | bytes 16777232 | tf_op jit(solution)/shard_map/gather | solution.py:82
  358.6 5.4 gather_fusion.3
  364.0 9.8 %gather_fusion.2 = f32[1024,4,128]{2,1,0:T(4,128)} fusion(f32[1536,4,128]{2,1,0:T(4,128)} %copy-done.2, s32[1024]{0:T(1024)S(1)} %fusion.22), kind=kCustom, calls=%fused_computation.2 | custom fusion | bytes 4198400 | tf_op jit(solution)/shard_map/gather | solution.py:117
  373.9 20.7 %fusion = (f32[4,1024]{1,0:T(4,128)S(1)}, f32[4,1024,1024]{1,2,0:T(8,128)S(1)}) fusion(pred[1024,1024]{0,1:T(8,128)(4,1)S(1)} %iota_compare_fusion.1, f32[1024,4,128]{2,1,0:T(4,128)S(1)} %gather_fusion.3, f32[1024,4,128]{2,1,0:T(4,128)} %gather_fusion.2), kind=kOutput, calls=%fused_computation.12 | convolution fusion | flops 6455029760 | bytes 22036480 | tf_op jit(solution)/shard_map/while/body/eval_jaxpr/qhd,khd->hqk/dot_general | solution.py:40
  394.5 5.7 copy-done
  400.2 3.6 fusion.1
  403.9 0.0 all-to-all-done
  403.9 5.4 gather_fusion.1
  409.3 18.2 %bitcast_divide_fusion = f32[1024,4,128]{0,2,1:T(8,128)} fusion(f32[1024,4]{0,1:T(4,128)S(1)} %bitcast.51, f32[4,1024,1024]{1,2,0:T(8,128)} %copy-done, f32[4,1024]{1,0:T(4,128)S(1)} %get-tuple-element.55, pred[1024,1024]{0,1:T(8,128)(4,1)S(1)} %iota_compare_fusion.1, f32[1024,4,128]{2,1,0:T(4,128)S(1)} %gather_fusion.1), kind=kOutput, calls=%fused_computation.38 | convolution fusion | flops 6455558144 | bytes 22052864 | tf_op jit(solution)/shard_map/while/body/eval_jaxpr/hqk,khd->qhd/dot_general | solution.py:48
  427.5 2.0 copy.25
  429.6 5.5 gather_fusion.5
  435.0 75.1 %all_to_all.34 = f32[1536,4,128]{2,1,0:T(4,128)S(1)} all-to-all(f32[1536,4,128]{2,1,0:T(4,128)} %gather_fusion.5), channel_id=1, replica_groups=mesh['seq'=8,'head'=4] {'seq'}, dimensions={0} | all-to-all | bytes 6291456 | tf_op jit(solution)/shard_map/all_to_all | solution.py:126
  510.2 7.9 %gather_fusion.6 = f32[1024,4,128]{2,1,0:T(4,128)} fusion(f32[1536,4,128]{2,1,0:T(4,128)S(1)} %all_to_all.34, s32[1024]{0:T(1024)S(1)} %get-tuple-element.38), kind=kCustom, calls=%fused_computation.6 | custom fusion | bytes 4198400 | tf_op jit(solution)/shard_map/gather | solution.py:127
  518.1 3.2 copy.55
  521.3 0.0 all-gather.2.cloned.1.call-update
  521.3 57.5 %all-gather.2.cloned.1.call-done = f32[1024,2048]{1,0:T(8,128)} async-done(((f32[1024,512]{1,0:T(8,128)}), f32[1024,2048]{1,0:T(8,128)}) %all-gather.2.cloned.1.call-update) | async-done | bytes 8388624 | tf_op jit(solution)/shard_map/all_gather | solution.py:128
  578.8 31.8 %fusion.34 = f32[1024,1024]{1,0:T(8,128)} fusion(f32[1024,2048]{1,0:T(8,128)} %all-gather.2.cloned.1.call-done, f32[2048,1024]{1,0:T(8,128)} %bitcast.45), kind=kOutput, calls=%fused_computation.86 | convolution fusion | flops 25769803776 | bytes 20971520 | tf_op jit(solution)/shard_map/dot_general | solution.py:129
  (19 shorter events, 0.2 us)
Async XLA Ops:
  16.6 57.2 %all-to-all-start.1 = ((s32[8,192,1]{1,2,0:T(1,128)}), s32[8,192,1]{1,2,0:T(1,128)S(1)}, u32[]{:S(2)}, u32[]{:S(2)}) async-start(s32[8,192,1]{1,2,0:T(1,128)} %all_to_all.27), calls=%async_computation.1 | async-start | bytes 16384 | tf_op jit(solution)/shard_map/all_to_all | solution.py:108
  28.7 3.0 copy-start.5
  41.2 2.2 copy-start.1
  43.4 3.1 copy-start.3
  149.9 73.8 %all-to-all-start.2 = ((f32[1536,4,128]{2,1,0:T(4,128)}), f32[1536,4,128]{2,1,0:T(4,128)S(1)}, u32[]{:S(2)}, u32[]{:S(2)}) async-start(f32[1536,4,128]{2,1,0:T(4,128)} %get-tuple-element.41), calls=%async_computation.2 | async-start | bytes 6291456 | tf_op jit(solution)/shard_map/all_to_all | solution.py:120
  223.8 1.7 copy-start.2
  225.5 178.4 %all-to-all-start = ((f32[1536,4,128]{2,1,0:T(4,128)}), f32[1536,4,128]{2,1,0:T(4,128)}, u32[]{:S(2)}, u32[]{:S(2)}) async-start(f32[1536,4,128]{2,1,0:T(4,128)} %get-tuple-element.40), calls=%async_computation | async-start | bytes 6291456 | tf_op jit(solution)/shard_map/all_to_all | solution.py:122
  230.0 348.7 %all-gather.2.cloned.1.call-start = ((), (), s32[]{:S(2)}) async-start(), calls=%async_computation.5 | async-start | bytes 10485760 | tf_op jit(solution)/shard_map/all_gather | solution.py:128
  251.9 41.7 %collective-permute-start.2 = (f32[512,1024]{1,0:T(8,128)}, f32[512,1024]{1,0:T(8,128)}, u32[]{:S(2)}, u32[]{:S(2)}) collective-permute-start(f32[512,1024]{1,0:T(8,128)} %bitcast.42), channel_id=1, source_target_pairs={{0,3},{1,0},{2,1},{3,2},{4,7},{5,4},{6,5},{7,6},{8,11},{9,8},{10,9... | collective-permute-start | bytes 6291464 | tf_op jit(solution)/shard_map/ppermute | solution.py:74
  255.4 86.2 %collective-permute-start.1 = (f32[512,1024]{1,0:T(8,128)}, f32[512,1024]{1,0:T(8,128)}, u32[]{:S(2)}, u32[]{:S(2)}) collective-permute-start(f32[512,1024]{1,0:T(8,128)} %fusion.9), channel_id=1, source_target_pairs={{0,2},{1,3},{2,0},{3,1},{4,6},{5,7},{6,4},{7,5},{8,10},{9,11},{10,... | collective-permute-start | bytes 6291464 | tf_op jit(solution)/shard_map/ppermute | solution.py:74
  256.9 2.1 copy-start.4
  258.7 86.4 %collective-permute-start = (f32[512,1024]{1,0:T(8,128)}, f32[512,1024]{1,0:T(8,128)}, u32[]{:S(2)}, u32[]{:S(2)}) collective-permute-start(f32[512,1024]{1,0:T(8,128)} %fusion.10), channel_id=1, source_target_pairs={{0,1},{1,2},{2,3},{3,0},{4,5},{5,6},{6,7},{7,4},{8,9},{9,10},{10,1... | collective-permute-start | bytes 6291464 | tf_op jit(solution)/shard_map/ppermute | solution.py:74
  394.5 5.7 copy-start
Sparse Core Ops, SparseCore 0:
  521.4 57.3 all-gather.1
where the time goes:
time: 622 us; the launch traced here: 618 us
  waiting for transfers between devices  196 us (32%)
  blocking collectives  151 us (24%)
  local copies, waits for them, and re-layouts  114 us (18%)
  matrix products  70.7 us (11%)
  other arithmetic  55 us (9%)
  starting transfers between devices  17.4 us (3%)
  between operations  14.2 us (2%)
    ppermute x3, waiting for transfers between devices, per_device(): lax.ppermute(jnp.take(weight_blocks, dest, axis=1), 'head', [(src, (src +...  79 us
    all_to_all x1, blocking collectives, per_device(): lax.all_to_all(send_k, 'seq', split_axis=0, concat_axis=0, tiled=True)  76.2 us
    all_to_all x1, blocking collectives, per_device(): lax.all_to_all(result[picked], 'seq', split_axis=0, concat_axis=0, tiled=...  75.1 us
    all_to_all x1, waiting for transfers between devices, per_device(): lax.all_to_all(send_q, 'seq', split_axis=0, concat_axis=0, tiled=True)  59.2 us
    all_gather x1, waiting for transfers between devices, per_device(): gathered = lax.all_gather(mixed, 'head', axis=1, tiled=True)  57.5 us
    dot_general x1, matrix products, per_device(): jnp.dot(gathered, weight_cols, precision=lax.Precision.HIGHEST, preferred...  31.8 us
    gather x3, local copies, waits for them, and re-layouts, place(): return pieces[where_from]  20.7 us
    dot_general x1, matrix products, cluster_attention(): jnp.einsum('qhd,khd->hqk', query_c, key_c, precision=lax.Precision.HIGHEST)  20.7 us
  transfers between devices with their start and end apart: 7, of which 5 were waited for; matrix products, arithmetic and copies ran while one was open for 24% of the time, Pallas kernels for 0%

commit v1 on v0

--- a/solution.py
+++ b/solution.py
@@ -12,6 +12,29 @@
 STRETCH = 4.0
 BETA_FAST = 32.0
 BETA_SLOW = 1.0
+
+
+def cut_along(x, dim, size):
+    shape = x.shape
+    pieces = x.reshape(*shape[:dim], size, shape[dim] // size, *shape[dim + 1 :])
+    return jnp.moveaxis(pieces, dim, 0)
+
+
+def in_order(blocks, dim):
+    blocks = jnp.moveaxis(blocks, 0, dim)
+    shape = blocks.shape
+    return blocks.reshape(*shape[:dim], shape[dim] * shape[dim + 1], *shape[dim + 2 :])
+
+
+def exchange_in_pairs(value, axis, split_dim, concat_dim):
+    size, here = (lax.axis_size(axis), lax.axis_index(axis))
+    blocks = cut_along(value, split_dim, size)
+    outs = [blocks[here]]
+    for turn in range(1, size):
+        sent = blocks[here ^ turn]
+        outs.append(lax.ppermute(sent, axis, [(i, i ^ turn) for i in range(size)]))
+    blocks = jnp.stack(outs)[here ^ jnp.arange(size)]
+    return in_order(blocks, concat_dim)
 
 
 def yarn_tables(token_pos, width):
@@ -117,7 +140,7 @@
         return pieces[where_from]
 
     received = (
-        lax.all_to_all(send_q, "seq", split_axis=0, concat_axis=0, tiled=True),
+        exchange_in_pairs(send_q, "seq", 0, 0),
         lax.all_to_all(send_k, "seq", split_axis=0, concat_axis=0, tiled=True),
         lax.all_to_all(send_v, "seq", split_axis=0, concat_axis=0, tiled=True),
     )

time: 622 us -> 573 us (0.921)
  blocking collectives: 151 us -> 85.9 us
  starting transfers between devices: 17.4 us -> 35.9 us
  waiting for transfers between devices: 196 us -> 179 us
  local copies, waits for them, and re-layouts: 114 us -> 128 us
    ppermute x0 -> x7, waiting for transfers between devices: none -> 81.7 us  [exchange_in_pairs(): outs.append(lax.ppermute(sent, axis, [(i, i ^ turn) for i in range(size)]))]
    ppermute x3, waiting for transfers between devices: 79 us -> 0.01 us  [per_device(): lax.ppermute(jnp.take(weight_blocks, dest, axis=1), 'head', [(src, (src +...]
    all_to_all x1 -> x0, blocking collectives: 76.2 us -> none  [per_device(): lax.all_to_all(send_k, 'seq', split_axis=0, concat_axis=0, tiled=True)]
    all_to_all x1, waiting for transfers between devices: 59.2 us -> 39.2 us  [per_device(): lax.all_to_all(send_k, 'seq', split_axis=0, concat_axis=0, tiled=True)]
    ppermute x0 -> x7, starting transfers between devices: none -> 14.8 us  [exchange_in_pairs(): outs.append(lax.ppermute(sent, axis, [(i, i ^ turn) for i in range(size)]))]
    all_to_all x1, blocking collectives: 75.1 us -> 85.9 us  [per_device(): lax.all_to_all(result[picked], 'seq', split_axis=0, concat_axis=0, tiled=...]
    unnamed x15 -> x21, local copies, waits for them, and re-layouts: 12.9 us -> 18.8 us
  transfers between devices with their start and end apart: 7 -> 14, of which waited for: 5 -> 8; matrix products, arithmetic and copies ran while one was open for 24% -> 25% of each run, Pallas kernels for 0% -> 0%
where the time goes in v1:
time: 573 us; the launch traced here: 569 us
  waiting for transfers between devices  179 us (31%)
  local copies, waits for them, and re-layouts  128 us (22%)
  blocking collectives  85.9 us (15%)
  matrix products  67.3 us (12%)
  other arithmetic  58.8 us (10%)
  starting transfers between devices  35.9 us (6%)
  between operations  13.9 us (2%)
    all_to_all x1, blocking collectives, per_device(): lax.all_to_all(result[picked], 'seq', split_axis=0, concat_axis=0, tiled=...  85.9 us
    ppermute x7, waiting for transfers between devices, exchange_in_pairs(): outs.append(lax.ppermute(sent, axis, [(i, i ^ turn) for i in range(size)]))  81.7 us
    all_gather x1, waiting for transfers between devices, per_device(): gathered = lax.all_gather(mixed, 'head', axis=1, tiled=True)  57.5 us
    all_to_all x1, waiting for transfers between devices, per_device(): lax.all_to_all(send_k, 'seq', split_axis=0, concat_axis=0, tiled=True)  39.2 us
    dot_general x1, matrix products, per_device(): jnp.dot(gathered, weight_cols, precision=lax.Precision.HIGHEST, preferred...  31.8 us
    gather x3, local copies, waits for them, and re-layouts, place(): return pieces[where_from]  21.1 us
    dynamic_slice x1, other arithmetic, per_device(): piece = weight_blocks[:, head_index]  20 us
    unnamed x21, local copies, waits for them, and re-layouts  18.8 us
  transfers between devices with their start and end apart: 14, of which 8 were waited for; matrix products, arithmetic and copies ran while one was open for 25% of the time, Pallas kernels for 0%

profile of v1, /device:TPU:0, one launch (start us, length us, event | category | flops | bytes accessed | tf_op | source)
XLA Modules:
  0.0 568.6 jit_solution(16265885518938642102)
XLA Ops:
  7.2 2.3 reduce-window.6
  10.0 0.7 fusion.18
  10.7 0.7 broadcast_clamp_fusion
  11.4 4.5 scatter_custom_fusion.1
  16.6 7.3 %all-to-all-start.1 = ((s32[8,192,1]{1,2,0:T(1,128)}), s32[8,192,1]{1,2,0:T(1,128)S(1)}, u32[]{:S(2)}, u32[]{:S(2)}) async-start(s32[8,192,1]{1,2,0:T(1,128)} %all_to_all.23), calls=%async_computation.1 | async-start | bytes 16384 | tf_op jit(solution)/shard_map/all_to_all | solution.py:131
  23.9 1.9 reshape.249
  25.8 2.9 reshape.250
  28.7 2.9 reshape.251
  31.6 4.5 scatter_custom_fusion
  36.1 4.6 slice_negate_fusion
  40.8 1.9 multiply_cosine_fusion
  43.0 3.0 fusion.7
  46.1 5.3 select_maximum_fusion
  52.2 12.0 %gather_fusion = f32[1536,12,128]{2,1,0:T(8,128)} fusion(f32[1025,12,128]{2,1,0:T(8,128)} %select_maximum_fusion, s32[2048]{0:T(1024)S(1)} %get-tuple-element.70), kind=kCustom, calls=%fused_computation | custom fusion | bytes 18880512 | tf_op jit(solution)/shard_map/gather | solution.py:126
  64.1 10.0 %fusion.34 = (f32[1536,4,128]{2,1,0:T(4,128)}, f32[1536,4,128]{2,1,0:T(4,128)S(1)}, f32[1536,4,128]{2,1,0:T(4,128)}) fusion(f32[1536,12,128]{2,1,0:T(8,128)} %gather_fusion), kind=kLoop, calls=%fused_computation.104 | loop fusion | bytes 18874368 | tf_op jit(solution)/shard_map/slice | solution.py:129
  74.1 6.3 %all-to-all-start.2 = ((f32[1536,4,128]{2,1,0:T(4,128)}), f32[1536,4,128]{2,1,0:T(4,128)}, u32[]{:S(2)}, u32[]{:S(2)}) async-start(f32[1536,4,128]{2,1,0:T(4,128)} %get-tuple-element.42), calls=%async_computation.2 | async-start | bytes 6291456 | tf_op jit(solution)/shard_map/all_to_all | solution.py:144
  80.4 10.8 %reshape.255 = f32[512,4,1024]{2,1,0:T(4,128)} reshape(f32[512,4096]{1,0:T(8,128)} %param.15) | data formatting | bytes 16777216 | tf_op jit(solution)/shard_map/reshape | solution.py:90
  91.3 20.0 %constant_dynamic-slice_fusion.2 = (f32[512,1,1024]{2,1,0:T(1,128)}, f32[512,1,1024]{2,1,0:T(1,128)}, f32[512,1,1024]{2,1,0:T(1,128)}, f32[512,1,1024]{2,1,0:T(1,128)}) fusion(f32[512,4,1024]{2,1,0:T(4,128)} %reshape.255, s32[]{:T(128)S(6)} %select_n.141, s32[]{:T(128)S(6)} %select_n.158, s32[]{:T(128)S(6)} %select_n.162, pred[]{:T(512)S(6)} %and.54, ...), kind=kLoop, calls=%fused_computation.89 | loop fusion | flops 524288 | bytes 16777232 | tf_op jit(solution)/shard_map/dynamic_slice | solution.py:94
  111.3 39.2 %all-to-all-done.2 = f32[1536,4,128]{2,1,0:T(4,128)} async-done(((f32[1536,4,128]{2,1,0:T(4,128)}), f32[1536,4,128]{2,1,0:T(4,128)}, u32[]{:S(2)}, u32[]{:S(2)}) %all-to-all-start.2) | async-done | bytes 3145760 | tf_op jit(solution)/shard_map/all_to_all | solution.py:144
  150.6 4.5 all-to-all-start
  155.1 3.5 fusion.10
  158.6 3.6 fusion.9
  162.2 1.5 collective-permute-start.8
  163.8 1.8 copy.56
  165.6 1.5 collective-permute-start.9
  167.0 3.4 copy.57
  171.7 1.5 dynamic-slice_bitcast_fusion
  173.2 1.8 collective-permute-start
  175.3 1.5 collective-permute-start.1
  176.9 6.3 %scatter_custom_fusion.2 = s32[1024]{0:T(1024)S(1)} fusion(s32[1536]{0:T(1024)} %get-tuple-element.37, s32[1536]{0:T(1024)S(1)} %iota.46, s32[]{:T(128)} %constant.138.clone.1), kind=kCustom, calls=%fused_computation.95 | custom fusion | bytes 4608 | tf_op jit(solution)/shard_map/scatter | solution.py:136
  183.2 7.8 %collective-permute-done = f32[192,4,128]{2,1,0:T(4,128)S(1)} collective-permute-done((f32[192,4,128]{2,1,0:T(4,128)}, f32[192,4,128]{2,1,0:T(4,128)S(1)}, u32[]{:S(2)}, u32[]{:S(2)}) %collective-permute-start) | collective-permute-done | bytes 393248 | tf_op jit(solution)/shard_map/ppermute | solution.py:35
  191.0 0.9 collective-permute-start.2
  191.9 0.8 bitcast_dynamic-update-slice_fusion.6
  192.7 23.6 %collective-permute-done.1 = f32[192,4,128]{2,1,0:T(4,128)S(1)} collective-permute-done((f32[192,4,128]{2,1,0:T(4,128)}, f32[192,4,128]{2,1,0:T(4,128)S(1)}, u32[]{:S(2)}, u32[]{:S(2)}) %collective-permute-start.1) | collective-permute-done | bytes 393248 | tf_op jit(solution)/shard_map/ppermute | solution.py:35
  216.3 4.0 collective-permute-start.3
  220.3 0.8 bitcast_dynamic-update-slice_fusion.5
  221.0 3.7 collective-permute-done.2
  224.7 4.9 collective-permute-start.4
  229.6 0.8 bitcast_dynamic-update-slice_fusion.4
  230.4 22.0 %collective-permute-done.3 = f32[192,4,128]{2,1,0:T(4,128)S(1)} collective-permute-done((f32[192,4,128]{2,1,0:T(4,128)}, f32[192,4,128]{2,1,0:T(4,128)S(1)}, u32[]{:S(2)}, u32[]{:S(2)}) %collective-permute-start.3) | collective-permute-done | bytes 393248 | tf_op jit(solution)/shard_map/ppermute | solution.py:35
  252.8 0.8 bitcast_dynamic-update-slice_fusion.3
  253.6 15.7 %collective-permute-done.4 = f32[192,4,128]{2,1,0:T(4,128)S(1)} collective-permute-done((f32[192,4,128]{2,1,0:T(4,128)}, f32[192,4,128]{2,1,0:T(4,128)S(1)}, u32[]{:S(2)}, u32[]{:S(2)}) %collective-permute-start.4) | collective-permute-done | bytes 393248 | tf_op jit(solution)/shard_map/ppermute | solution.py:35
  269.3 1.3 collective-permute-start.6
  270.6 0.8 bitcast_dynamic-update-slice_fusion.2
  271.4 0.8 bitcast_dynamic-update-slice_fusion.1
  272.1 8.9 %collective-permute-done.6 = f32[192,4,128]{2,1,0:T(4,128)S(1)} collective-permute-done((f32[192,4,128]{2,1,0:T(4,128)S(1)}, f32[192,4,128]{2,1,0:T(4,128)S(1)}, u32[]{:S(2)}, u32[]{:S(2)}) %collective-permute-start.6) | collective-permute-done | bytes 393248 | tf_op jit(solution)/shard_map/ppermute | solution.py:35
  281.1 0.8 bitcast_dynamic-update-slice_fusion
  281.9 5.9 %gather_fusion.2 = f32[8,192,4,128]{3,2,1,0:T(4,128)} fusion(f32[8,192,4,128]{3,2,1,0:T(4,128)} %bitcast_dynamic-update-slice_fusion, s32[1024]{0:T(1024)} %pad_clamp_fusion.3), kind=kCustom, calls=%fused_computation.2 | custom fusion | bytes 6291488 | tf_op jit(solution)/shard_map/gather | solution.py:36
  287.8 5.4 gather_fusion.3
  293.3 6.0 %pad_maximum_fusion = f32[4,512,1024]{2,1,0:T(8,128)} fusion(f32[1,512,1024]{2,1,0:T(8,128)} %bitcast.27, f32[1,512,1024]{2,1,0:T(8,128)} %bitcast.26, f32[1,512,1024]{2,1,0:T(8,128)} %bitcast.24, f32[1,512,1024]{2,1,0:T(8,128)} %bitcast.82), kind=kLoop, calls=%fused_computation.19 | loop fusion | flops 6291456 | bytes 16777216 | tf_op jit(solution)/shard_map/stack | solution.py:103
  299.3 7.8 %gather_fusion.5 = f32[4,512,1024]{2,1,0:T(8,128)} fusion(f32[4,512,1024]{2,1,0:T(8,128)} %pad_maximum_fusion, s32[1024]{0:T(1024)} %pad_clamp_fusion.2), kind=kCustom, calls=%fused_computation.5 | custom fusion | bytes 16777232 | tf_op jit(solution)/shard_map/gather | solution.py:105
  307.1 10.2 %gather_fusion.4 = f32[1024,4,128]{2,1,0:T(4,128)} fusion(f32[1536,4,128]{2,1,0:T(4,128)} %all-to-all-done.2, s32[1024]{0:T(1024)S(1)} %fusion.22), kind=kCustom, calls=%fused_computation.4 | custom fusion | bytes 4198400 | tf_op jit(solution)/shard_map/gather | solution.py:140
  317.3 17.5 %fusion = (f32[4,1024]{1,0:T(4,128)S(1)}, f32[4,1024,1024]{1,2,0:T(8,128)S(1)}) fusion(pred[1024,1024]{0,1:T(8,128)(4,1)S(1)} %iota_compare_fusion.1, f32[1024,4,128]{2,1,0:T(4,128)} %gather_fusion.4, f32[1024,4,128]{2,1,0:T(4,128)S(1)} %gather_fusion.3), kind=kOutput, calls=%fused_computation.13 | convolution fusion | flops 6455029760 | bytes 22036480 | tf_op jit(solution)/shard_map/while/body/eval_jaxpr/qhd,khd->hqk/dot_general | solution.py:63
  334.8 5.7 %copy-done = f32[4,1024,1024]{1,2,0:T(8,128)} copy-done((f32[4,1024,1024]{1,2,0:T(8,128)}, f32[4,1024,1024]{1,2,0:T(8,128)S(1)}, u32[]{:S(2)}) %copy-start) | copy-done | bytes 16777240
  340.5 3.6 fusion.1
  344.2 5.4 gather_fusion.1
  349.6 17.9 %bitcast_divide_fusion = f32[1024,4,128]{0,2,1:T(8,128)} fusion(f32[1024,4]{0,1:T(4,128)S(1)} %bitcast.85, f32[4,1024,1024]{1,2,0:T(8,128)} %copy-done, f32[4,1024]{1,0:T(4,128)S(1)} %get-tuple-element.63, pred[1024,1024]{0,1:T(8,128)(4,1)S(1)} %iota_compare_fusion.1, f32[1024,4,128]{2,1,0:T(4,128)S(1)} %gather_fusion.1), kind=kOutput, calls=%fused_computation.39 | convolution fusion | flops 6455558144 | bytes 22052864 | tf_op jit(solution)/shard_map/while/body/eval_jaxpr/hqk,khd->qhd/dot_general | solution.py:71
  367.5 2.0 copy.25
  369.6 5.7 %gather_fusion.6 = f32[1536,4,128]{2,1,0:T(4,128)} fusion(f32[1024,4,128]{2,1,0:T(4,128)S(1)} %copy.25, s32[2048]{0:T(1024)S(1)} %get-tuple-element.69), kind=kCustom, calls=%fused_computation.6 | custom fusion | bytes 6297600 | tf_op jit(solution)/shard_map/gather | solution.py:149
  375.3 85.9 %all_to_all.28 = f32[1536,4,128]{2,1,0:T(4,128)S(1)} all-to-all(f32[1536,4,128]{2,1,0:T(4,128)} %gather_fusion.6), channel_id=1, replica_groups=mesh['seq'=8,'head'=4] {'seq'}, dimensions={0} | all-to-all | bytes 6291456 | tf_op jit(solution)/shard_map/all_to_all | solution.py:149
  461.1 7.9 %gather_fusion.7 = f32[1024,4,128]{2,1,0:T(4,128)} fusion(f32[1536,4,128]{2,1,0:T(4,128)S(1)} %all_to_all.28, s32[1024]{0:T(1024)S(1)} %get-tuple-element.38), kind=kCustom, calls=%fused_computation.7 | custom fusion | bytes 4198400 | tf_op jit(solution)/shard_map/gather | solution.py:150
  469.1 3.1 copy.55
  472.2 57.5 %all-gather.2.cloned.1.call-done = f32[1024,2048]{1,0:T(8,128)} async-done(((f32[1024,512]{1,0:T(8,128)}), f32[1024,2048]{1,0:T(8,128)}) %all-gather.2.cloned.1.call-update) | async-done | bytes 8388624 | tf_op jit(solution)/shard_map/all_gather | solution.py:151
  529.7 31.8 %fusion.35 = f32[1024,1024]{1,0:T(8,128)} fusion(f32[1024,2048]{1,0:T(8,128)} %all-gather.2.cloned.1.call-done, f32[2048,1024]{1,0:T(8,128)} %bitcast.79), kind=kOutput, calls=%fused_computation.105 | convolution fusion | flops 25769803776 | bytes 20971520 | tf_op jit(solution)/shard_map/dot_general | solution.py:152
  (42 shorter events, 5.0 us)
Async XLA Ops:
  16.6 34.8 %all-to-all-start.1 = ((s32[8,192,1]{1,2,0:T(1,128)}), s32[8,192,1]{1,2,0:T(1,128)S(1)}, u32[]{:S(2)}, u32[]{:S(2)}) async-start(s32[8,192,1]{1,2,0:T(1,128)} %all_to_all.23), calls=%async_computation.1 | async-start | bytes 16384 | tf_op jit(solution)/shard_map/all_to_all | solution.py:131
  23.8 4.9 copy-start.5
  40.8 2.2 copy-start.1
  43.0 3.1 copy-start.2
  74.1 76.5 %all-to-all-start.2 = ((f32[1536,4,128]{2,1,0:T(4,128)}), f32[1536,4,128]{2,1,0:T(4,128)}, u32[]{:S(2)}, u32[]{:S(2)}) async-start(f32[1536,4,128]{2,1,0:T(4,128)} %get-tuple-element.42), calls=%async_computation.2 | async-start | bytes 6291456 | tf_op jit(solution)/shard_map/all_to_all | solution.py:144
  150.6 193.6 %all-to-all-start = ((f32[1536,4,128]{2,1,0:T(4,128)}), f32[1536,4,128]{2,1,0:T(4,128)}, u32[]{:S(2)}, u32[]{:S(2)}) async-start(f32[1536,4,128]{2,1,0:T(4,128)} %get-tuple-element.40), calls=%async_computation | async-start | bytes 6291456 | tf_op jit(solution)/shard_map/all_to_all | solution.py:145
  155.1 374.6 %all-gather.2.cloned.1.call-start = ((), (), s32[]{:S(2)}) async-start(), calls=%async_computation.4 | async-start | bytes 10485760 | tf_op jit(solution)/shard_map/all_gather | solution.py:151
  158.6 134.6 %collective-permute-start.7 = (f32[512,1024]{1,0:T(8,128)}, f32[512,1024]{1,0:T(8,128)}, u32[]{:S(2)}, u32[]{:S(2)}) collective-permute-start(f32[512,1024]{1,0:T(8,128)} %fusion.10), channel_id=1, source_target_pairs={{0,1},{1,2},{2,3},{3,0},{4,5},{5,6},{6,7},{7,4},{8,9},{9,10},{10,1... | collective-permute-start | bytes 6291464 | tf_op jit(solution)/shard_map/ppermute | solution.py:97
  158.6 5.1 copy-start.3
  162.2 131.0 %collective-permute-start.8 = (f32[512,1024]{1,0:T(8,128)}, f32[512,1024]{1,0:T(8,128)}, u32[]{:S(2)}, u32[]{:S(2)}) collective-permute-start(f32[512,1024]{1,0:T(8,128)} %fusion.9), channel_id=1, source_target_pairs={{0,2},{1,3},{2,0},{3,1},{4,6},{5,7},{6,4},{7,5},{8,10},{9,11},{10,... | collective-permute-start | bytes 6291464 | tf_op jit(solution)/shard_map/ppermute | solution.py:97
  165.6 127.7 %collective-permute-start.9 = (f32[512,1024]{1,0:T(8,128)}, f32[512,1024]{1,0:T(8,128)}, u32[]{:S(2)}, u32[]{:S(2)}) collective-permute-start(f32[512,1024]{1,0:T(8,128)} %bitcast.74), channel_id=1, source_target_pairs={{0,3},{1,0},{2,1},{3,2},{4,7},{5,4},{6,5},{7,6},{8,11},{9,8},{10,9... | collective-permute-start | bytes 6291464 | tf_op jit(solution)/shard_map/ppermute | solution.py:97
  173.2 79.2 %copy-start.4 = (f32[192,4,128]{2,1,0:T(4,128)S(1)}, f32[192,4,128]{2,1,0:T(4,128)}, u32[]{:S(2)}) copy-start(f32[192,4,128]{2,1,0:T(4,128)} %get-tuple-element.48) | copy-start | bytes 1179652
  173.2 17.9 %collective-permute-start = (f32[192,4,128]{2,1,0:T(4,128)}, f32[192,4,128]{2,1,0:T(4,128)S(1)}, u32[]{:S(2)}, u32[]{:S(2)}) collective-permute-start(f32[192,4,128]{2,1,0:T(4,128)} %get-tuple-element.53), channel_id=1, source_target_pairs={{0,4},{4,0},{8,12},{12,8},{16,20},{20,16},{24,28},{28,24},{1,5},{5... | collective-permute-start | bytes 1179656 | tf_op jit(solution)/shard_map/ppermute | solution.py:35
  175.3 40.9 %collective-permute-start.1 = (f32[192,4,128]{2,1,0:T(4,128)}, f32[192,4,128]{2,1,0:T(4,128)S(1)}, u32[]{:S(2)}, u32[]{:S(2)}) collective-permute-start(f32[192,4,128]{2,1,0:T(4,128)} %get-tuple-element.52), channel_id=1, source_target_pairs={{0,8},{4,12},{8,0},{12,4},{16,24},{20,28},{24,16},{28,20},{1,9},{5... | collective-permute-start | bytes 1179656 | tf_op jit(solution)/shard_map/ppermute | solution.py:35
  191.0 33.6 %collective-permute-start.2 = (f32[192,4,128]{2,1,0:T(4,128)}, f32[192,4,128]{2,1,0:T(4,128)S(1)}, u32[]{:S(2)}, u32[]{:S(2)}) collective-permute-start(f32[192,4,128]{2,1,0:T(4,128)} %get-tuple-element.51), channel_id=1, source_target_pairs={{0,12},{4,8},{8,4},{12,0},{16,28},{20,24},{24,20},{28,16},{1,13},{... | collective-permute-start | bytes 1179656 | tf_op jit(solution)/shard_map/ppermute | solution.py:35
  216.3 36.1 %collective-permute-start.3 = (f32[192,4,128]{2,1,0:T(4,128)}, f32[192,4,128]{2,1,0:T(4,128)S(1)}, u32[]{:S(2)}, u32[]{:S(2)}) collective-permute-start(f32[192,4,128]{2,1,0:T(4,128)} %get-tuple-element.50), channel_id=1, source_target_pairs={{0,16},{4,20},{8,24},{12,28},{16,0},{20,4},{24,8},{28,12},{1,17},{... | collective-permute-start | bytes 1179656 | tf_op jit(solution)/shard_map/ppermute | solution.py:35
  224.7 44.6 %collective-permute-start.4 = (f32[192,4,128]{2,1,0:T(4,128)}, f32[192,4,128]{2,1,0:T(4,128)S(1)}, u32[]{:S(2)}, u32[]{:S(2)}) collective-permute-start(f32[192,4,128]{2,1,0:T(4,128)} %get-tuple-element.49), channel_id=1, source_target_pairs={{0,20},{4,16},{8,28},{12,24},{16,4},{20,0},{24,12},{28,8},{1,21},{... | collective-permute-start | bytes 1179656 | tf_op jit(solution)/shard_map/ppermute | solution.py:35
  252.4 19.0 %collective-permute-start.5 = (f32[192,4,128]{2,1,0:T(4,128)S(1)}, f32[192,4,128]{2,1,0:T(4,128)S(1)}, u32[]{:S(2)}, u32[]{:S(2)}) collective-permute-start(f32[192,4,128]{2,1,0:T(4,128)S(1)} %copy-done.4), channel_id=1, source_target_pairs={{0,24},{4,28},{8,16},{12,20},{16,8},{20,12},{24,0},{28,4},{1,25},{... | collective-permute-start | bytes 1179656 | tf_op jit(solution)/shard_map/ppermute | solution.py:35
  269.3 11.8 %collective-permute-start.6 = (f32[192,4,128]{2,1,0:T(4,128)S(1)}, f32[192,4,128]{2,1,0:T(4,128)S(1)}, u32[]{:S(2)}, u32[]{:S(2)}) collective-permute-start(f32[192,4,128]{2,1,0:T(4,128)S(1)} %get-tuple-element.47), channel_id=1, source_target_pairs={{0,28},{4,24},{8,20},{12,16},{16,12},{20,8},{24,4},{28,0},{1,29},{... | collective-permute-start | bytes 1179656 | tf_op jit(solution)/shard_map/ppermute | solution.py:35
  334.8 5.7 %copy-start = (f32[4,1024,1024]{1,2,0:T(8,128)}, f32[4,1024,1024]{1,2,0:T(8,128)S(1)}, u32[]{:S(2)}) copy-start(f32[4,1024,1024]{1,2,0:T(8,128)S(1)} %get-tuple-element.64) | copy-start | bytes 50331652
Sparse Core Ops, SparseCore 0:
  472.3 57.3 all-gather.1
